TPU v7x, 128 devices: a whole 4x4x4 slice. The times are simulated.
128 devices in a mesh: pipe: 4 (over x_hi, core), dp: 16 (over y, z), tensor: 2 (over x_lo).
Axes of the slice: x: 4 (x_hi: 2, x_lo: 2; x = x_hi * 2 + x_lo), y: 4, z: 4, core: 2. Of those that a mesh axis runs over, the one named last changes fastest.
Arguments:
- hidden_states: bfloat16 [4, 4096, 8192], P('pipe', 'dp'), may hold values from -60 to 60
- norm_gain: bfloat16 [4, 8192], P('pipe'), may hold values from 0.5 to 2
- key_weight: bfloat16 [4, 8192, 512], P('pipe', 'dp', 'tensor'), may hold values from -0.0625 to 0.0625
- value_weight: bfloat16 [4, 8192, 512], P('pipe', 'dp', 'tensor'), may hold values from -0.0625 to 0.0625
- queries: bfloat16 [4, 4096, 4096], P('pipe', 'dp', 'tensor'), may hold values from -128 to 128
- context_cotangent: bfloat16 [4, 4096, 4096], P('pipe', 'dp', 'tensor'), may hold values from -96 to 96
- lengths: int32 [4, 16], P('pipe', 'dp'), may hold values from 64 to 256, as said below
- policy_logp: float32 [4, 16], P('pipe', 'dp'), may hold values from -90 to -30
- reference_logp: float32 [4, 16], P('pipe', 'dp'), may hold values from -90 to -30
Outputs:
- key_weight_grad: bfloat16 [4, 8192, 512], P('pipe', 'dp', 'tensor')
- value_weight_grad: bfloat16 [4, 8192, 512], P('pipe', 'dp', 'tensor')
- lower_cotangent: bfloat16 [4, 4096, 8192], P('pipe', 'dp')
Inputs may be any that keep to these rules, and one draw needn't show every extreme that they name: `lengths`: each sequence's live tokens; positions at or beyond it are padding.
All inputs are finite; a program needn't handle non-finite values.
Results may differ from a plain program's by a relative error of at most 0.015.
The roundings to bfloat16 on the way count: a program that leaves them out, or rounds other values in their place, can miss the bound.
Values may be sent and summed in bfloat16 or wider, within the bound.
No kernel may reach another device: no remote copies, remote signals or barrier semaphores. Data moves between devices by JAX's collectives and lax.ppermute only.
A program may use at most 128 MiB of HBM per device.

v0:
```python
import math
import jax
import jax.numpy as jnp
from jax import lax
from jax.sharding import PartitionSpec as P

HD = 128
npo_beta = 0.1
norm_eps = 1e-05
rope_base = 500000.0


def shifted(value, axis, steps):
    count = lax.axis_size(axis)
    leading, last = (max(0, -steps), min(count, count - steps))
    return lax.ppermute(value, axis, [(source, source + steps) for source in range(leading, last)])


def rope_tables(length, head_dim):
    positions = jnp.arange(length).astype(jnp.float32)
    freq_index = jnp.arange(head_dim // 2).astype(jnp.float32)
    inverse = 1.0 / rope_base ** (2.0 * freq_index / head_dim)
    angles = positions[:, None] * inverse[None, :]
    cosine = jnp.concatenate([jnp.cos(angles), jnp.cos(angles)], axis=1)
    sine = jnp.concatenate([jnp.sin(angles), jnp.sin(angles)], axis=1)
    return (cosine, sine)


def rotate_half(values):
    half = values.shape[-1] // 2
    return jnp.concatenate([-values[..., half:], values[..., :half]], axis=-1)


def rotate_back(values):
    half = values.shape[-1] // 2
    return jnp.concatenate([values[..., half:], -values[..., :half]], axis=-1)


def sequence_grads(query_seq, key_seq, value_seq, cotan_seq, length_seq, cosine, sine):
    seq_len, kv_heads, head_dim = key_seq.shape
    group = query_seq.shape[1] // kv_heads
    scale = 1.0 / math.sqrt(head_dim)
    query_g = query_seq.reshape(seq_len, kv_heads, group, head_dim)
    cotan_g = cotan_seq.reshape(seq_len, kv_heads, group, head_dim)
    scores = (
        jnp.einsum("ikgd,jkd->kgij", query_g, key_seq, preferred_element_type=jnp.float32) * scale
    )
    row_pos = jnp.arange(seq_len)[:, None]
    col_pos = jnp.arange(seq_len)[None, :]
    allowed = (col_pos <= row_pos) & (col_pos < length_seq)
    scores = jnp.where(allowed, scores, -1e30)
    highest = jnp.max(scores, axis=-1, keepdims=True)
    expd = jnp.where(allowed, jnp.exp(scores - highest), 0.0)
    probs = expd / jnp.sum(expd, axis=-1, keepdims=True)
    probs_low = probs.astype(jnp.bfloat16)
    value_grad = jnp.einsum(
        "kgij,ikgd->jkd", probs_low, cotan_g, preferred_element_type=jnp.float32
    ).astype(jnp.bfloat16)
    prob_grad = jnp.einsum("ikgd,jkd->kgij", cotan_g, value_seq, preferred_element_type=jnp.float32)
    centre = jnp.sum(probs * prob_grad, axis=-1, keepdims=True)
    score_grad = (probs * (prob_grad - centre) * scale).astype(jnp.bfloat16)
    rotated_grad = jnp.einsum(
        "kgij,ikgd->jkd", score_grad, query_g, preferred_element_type=jnp.float32
    )
    key_grad = rotated_grad * cosine[:, None, :] + rotate_back(rotated_grad * sine[:, None, :])
    return (key_grad.astype(jnp.bfloat16), value_grad)


def norm_backward(normed_grad, gain_f, nhat, inv_rms):
    gain_grad_in = normed_grad * gain_f
    centre = jnp.mean(gain_grad_in * nhat, axis=-1, keepdims=True)
    return ((gain_grad_in - nhat * centre) * inv_rms).astype(jnp.bfloat16)


def on_device(
    hidden_states,
    norm_gain,
    key_weight,
    value_weight,
    queries,
    context_cotangent,
    lengths,
    policy_logp,
    reference_logp,
):
    both_full = lax.all_gather(
        jnp.stack([key_weight[0], value_weight[0]]), "dp", axis=1, tiled=True
    )
    key_full, value_full = (both_full[0], both_full[1])
    hidden = hidden_states[0]
    gain_f = norm_gain[0].astype(jnp.float32)
    tok_rows = hidden.shape[0]
    seq_count = lengths.shape[1]
    seq_len = tok_rows // seq_count
    kv_cols = key_full.shape[1]
    kv_local = kv_cols // HD
    q_local = queries.shape[2] // HD
    hidden_f = hidden.astype(jnp.float32)
    inv_rms = lax.rsqrt(jnp.mean(hidden_f * hidden_f, axis=-1, keepdims=True) + norm_eps)
    nhat = hidden_f * inv_rms
    normed = (nhat * gain_f).astype(jnp.bfloat16)
    projected = jnp.einsum("td,wdc->wtc", normed, both_full, preferred_element_type=jnp.float32)
    key_raw = projected[0]
    values = projected[1].astype(jnp.bfloat16)
    cosine, sine = rope_tables(seq_len, HD)
    key_four = key_raw.reshape(seq_count, seq_len, kv_local, HD)
    keys = (
        key_four * cosine[None, :, None, :] + rotate_half(key_four) * sine[None, :, None, :]
    ).astype(jnp.bfloat16)
    total_seqs = seq_count * lax.axis_size("dp")
    seq_weight = 2.0 * jax.nn.sigmoid(npo_beta * (policy_logp[0] - reference_logp[0])) / total_seqs
    live = jnp.arange(seq_len)[None, :] < lengths[0][:, None]
    factor = jnp.where(live, seq_weight[:, None], 0.0)
    scaled = (
        context_cotangent[0].reshape(seq_count, seq_len, q_local, HD).astype(jnp.float32)
        * factor[:, :, None, None]
    ).astype(jnp.bfloat16)

    def one_sequence(items):
        return sequence_grads(items[0], items[1], items[2], items[3], items[4], cosine, sine)

    key_grad, value_grad = lax.map(
        one_sequence,
        (
            queries[0].reshape(seq_count, seq_len, q_local, HD),
            keys,
            values.reshape(seq_count, seq_len, kv_local, HD),
            scaled,
            lengths[0],
        ),
    )
    key_grad = key_grad.reshape(tok_rows, kv_cols)
    value_grad = value_grad.reshape(tok_rows, kv_cols)
    combined = jnp.concatenate([key_grad, value_grad], axis=1)
    grad_total = lax.psum_scatter(
        lax.dot_general(
            normed, combined, (((0,), (0,)), ((), ())), preferred_element_type=jnp.float32
        ).astype(jnp.bfloat16),
        "dp",
        scatter_dimension=0,
        tiled=True,
    )
    both_grads = jnp.stack([key_grad, value_grad])
    n_pipe = lax.axis_size("pipe")
    n_tensor = lax.axis_size("tensor")
    sizes = [tok_rows // 4, tok_rows * 5 // 16, tok_rows * 5 // 16, tok_rows // 8]
    bounds = [sum(sizes[:c]) for c in range(len(sizes) + 1)]
    chunks = len(sizes)
    exchange_steps = [
        [
            (p * n_tensor + t, p * n_tensor + (t + step) % n_tensor)
            for p in range(1, n_pipe)
            for t in range(n_tensor)
        ]
        for step in range(1, n_tensor)
    ]
    shift_pairs = [
        ((p + 1) * n_tensor + (t if (p + 1) // 2 == p // 2 else n_tensor - 1 - t), p * n_tensor + t)
        for p in range(n_pipe - 1)
        for t in range(n_tensor)
    ]
    lowers = []
    held = None
    for c in range(chunks):
        sl = slice(bounds[c], bounds[c + 1])
        part = jnp.einsum(
            "wtc,wdc->td", both_grads[:, sl], both_full, preferred_element_type=jnp.float32
        )
        part_low = part.astype(jnp.bfloat16)
        if held is not None:
            if len(lowers) > 0:
                part_low, held, lowers[-1] = lax.optimization_barrier((part_low, held, lowers[-1]))
            else:
                part_low, held = lax.optimization_barrier((part_low, held))
            lowers.append(lax.ppermute(held, ("pipe", "tensor"), shift_pairs))
        normed_grad = part_low.astype(jnp.float32)
        for pairs in exchange_steps:
            normed_grad = normed_grad + lax.ppermute(part_low, ("pipe", "tensor"), pairs).astype(
                jnp.float32
            )
        held = norm_backward(normed_grad, gain_f, nhat[sl], inv_rms[sl])
    lowers.append(lax.ppermute(held, ("pipe", "tensor"), shift_pairs))
    lower = jnp.concatenate(lowers, axis=0)
    return (grad_total[:, :kv_cols][None], grad_total[:, kv_cols:][None], lower[None])


def solution(mesh):
    in_specs = (
        P("pipe", "dp", None),
        P("pipe", None),
        P("pipe", "dp", "tensor"),
        P("pipe", "dp", "tensor"),
        P("pipe", "dp", "tensor"),
        P("pipe", "dp", "tensor"),
        P("pipe", "dp"),
        P("pipe", "dp"),
        P("pipe", "dp"),
    )
    out_specs = (P("pipe", "dp", "tensor"), P("pipe", "dp", "tensor"), P("pipe", "dp", None))
    return jax.shard_map(
        on_device, mesh=mesh, in_specs=in_specs, out_specs=out_specs, check_vma=False
    )
```

profile of v0, /device:TPU:1, one launch (start us, length us, event | category | flops | bytes accessed | tf_op | source)
XLA Modules:
  0.0 254.6 jit_solution(5297577957536231163)
XLA Ops:
  17.3 3.1 %fusion.6 = f32[256]{0:T(256)S(1)} fusion(bf16[1,256,8192]{2,1,0:T(8,128)(2,1)} %param.9), kind=kLoop, calls=%fused_computation.13 | loop fusion | flops 6291200 | bytes 4195328 | tf_op jit(solution)/shard_map/reduce_sum | solution.py:99
  20.5 71.1 %all-gather.2.cloned.1.call-done = bf16[2,8192,256]{1,2,0:T(8,128)(2,1)} async-done(((bf16[2,512,256]{1,2,0:T(8,128)(2,1)}), bf16[2,8192,256]{1,2,0:T(8,128)(2,1)}) %all-gather.2.cloned.1.call-update) | async-done | bytes 8388624 | tf_op jit(solution)/shard_map/all_gather | solution.py:86
  91.7 7.0 %fusion.20 = f32[2,256,256]{1,2,0:T(8,128)S(1)} fusion(bf16[2,8192,256]{1,2,0:T(8,128)(2,1)} %all-gather.2.cloned.1.call-done, f32[8192]{0:T(1024)S(1)} %bitcast.125, bf16[1,256,8192]{2,1,0:T(8,128)(2,1)} %param.9, f32[256]{0:T(256)S(1)} %add_rsqrt_fusion), kind=kOutput, calls=%fused_computation.44 | convolution fusion | flops 2155872256 | bytes 13140992 | tf_op jit(solution)/shard_map/td,wdc->wtc/dot_general | solution.py:102
  99.9 5.3 %fusion.60 = (f32[2,8,256]{2,1,0:T(8,128)S(1)}, f32[2,8,256,256]{2,3,1,0:T(8,128)}) fusion(pred[256,256]{0,1:T(8,128)(4,1)S(1)} %fusion.39, bf16[256,2,8,128]{0,3,2,1:T(8,128)(2,1)} %bitcast.137, f32[256,2,64]{2,0,1:T(8,128)S(1)} %bitcast.142, f32[256,2,64]{2,0,1:T(8,128)} %negate_bitcast_fusion, f32[256,2,128]{2,0,1:T(8,128)S(1)} %copy.15, ...), kind=kOutput, calls=%fused_computation.107 | convolution fusion | flops 274006272 | bytes 6111232 | tf_op jit(solution)/shard_map/while/body/eval_jaxpr/sub | solution.py:53
  105.1 3.0 %fusion.27 = bf16[2,128,256]{2,1,0:T(8,128)(2,1)S(1)} fusion(f32[256,2,8,128]{0,3,2,1:T(8,128)S(1)} %bitcast.123, f32[256]{0:T(256)S(1)} %broadcast_select_fusion, f32[2,8,256,256]{2,3,1,0:T(8,128)} %get-tuple-element.60, f32[2,8,256]{2,1,0:T(8,128)S(1)} %get-tuple-element.59), kind=kOutput, calls=%fused_computation.47 | convolution fusion | flops 271646720 | bytes 6439936 | tf_op jit(solution)/shard_map/while/body/eval_jaxpr/kgij,ikgd->jkd/dot_general | solution.py:56
  108.3 2.7 %fusion.30 = f32[2,256,256,8]{2,1,3,0:T(8,128)} fusion(bf16[256,2,128,1]{0,2,3,1:T(8,128)(2,1)S(1)} %bitcast.139, f32[256,2,8,128]{0,3,2,1:T(8,128)S(1)} %bitcast.124, f32[256]{0:T(256)S(1)} %broadcast_select_fusion), kind=kOutput, calls=%fused_computation.52 | convolution fusion | flops 269484032 | bytes 6423552 | tf_op jit(solution)/shard_map/while/body/eval_jaxpr/ikgd,jkd->kgij/dot_general | solution.py:59
  111.0 7.5 %fusion.23 = f32[2,256,128]{1,2,0:T(8,128)S(1)} fusion(bf16[256,2,8,128]{0,3,2,1:T(8,128)(2,1)} %bitcast.138, f32[2,256,256,8]{2,1,3,0:T(8,128)} %fusion.30, f32[2,8,256,256]{2,3,1,0:T(8,128)} %get-tuple-element.60, f32[2,8,256]{2,1,0:T(8,128)S(1)} %get-tuple-element.59), kind=kOutput, calls=%fused_computation.45 | convolution fusion | flops 275779840 | bytes 9715712 | tf_op jit(solution)/shard_map/while/body/eval_jaxpr/kgij,ikgd->jkd/dot_general | solution.py:62
  118.7 5.1 %fusion.4 = bf16[64,8192]{1,0:T(8,128)(2,1)S(1)} fusion(bf16[2,8192,256]{1,2,0:T(8,128)(2,1)} %all-gather.2.cloned.1.call-done, bf16[1,256,256]{2,1,0:T(8,128)(2,1)S(1)} %copy.26, bf16[1,256,256]{2,1,0:T(8,128)(2,1)S(1)} %copy.27), kind=kOutput, calls=%fused_computation.10 | convolution fusion | flops 537427968 | bytes 9699328 | tf_op jit(solution)/shard_map/wtc,wdc->td/dot_general | solution.py:166
  123.8 3.3 %collective-permute-start = (bf16[64,8192]{1,0:T(8,128)(2,1)S(1)}, bf16[64,8192]{1,0:T(8,128)(2,1)S(1)}, u32[]{:S(2)}, u32[]{:S(2)}) collective-permute-start(bf16[64,8192]{1,0:T(8,128)(2,1)S(1)} %fusion.4), channel_id=1, source_target_pairs={{32,33},{33,32},{64,65},{65,64},{96,97},{97,96},{34,35},{35,34},{6... | collective-permute-start | bytes 3145736 | tf_op jit(solution)/shard_map/ppermute | solution.py:178
  127.1 5.8 %convolution_convert_fusion = bf16[8192,512]{1,0:T(8,128)(2,1)} fusion(f32[8192]{0:T(1024)S(1)} %bitcast.126, bf16[256,256]{0,1:T(8,128)(2,1)S(1)} %bitcast.144, bf16[256,256]{0,1:T(8,128)(2,1)S(1)} %bitcast.141, bf16[1,256,8192]{2,1,0:T(8,128)(2,1)S(1)} %copy-done, f32[256]{0:T(256)S(1)} %add_rsqrt_fusion), kind=kOutput, calls=%fused_computation.2 | convolution fusion | flops 2160590848 | bytes 12878848 | tf_op jit(solution)/shard_map/dot_general | solution.py:136
  132.9 3.3 %convert_multiply_fusion = f32[256,8192]{1,0:T(8,128)S(1)} fusion(bf16[1,256,8192]{2,1,0:T(8,128)(2,1)} %param.9, f32[256]{0:T(256)S(1)} %add_rsqrt_fusion), kind=kLoop, calls=%fused_computation.3 | loop fusion | flops 4194304 | bytes 12583936 | tf_op jit(solution)/shard_map/mul | solution.py:100
  136.2 5.1 %fusion.3 = bf16[80,8192]{1,0:T(8,128)(2,1)S(1)} fusion(bf16[2,8192,256]{1,2,0:T(8,128)(2,1)} %all-gather.2.cloned.1.call-done, bf16[1,256,256]{2,1,0:T(8,128)(2,1)S(1)} %copy.26, bf16[1,256,256]{2,1,0:T(8,128)(2,1)S(1)} %copy.27), kind=kOutput, calls=%fused_computation.9 | convolution fusion | flops 671784960 | bytes 9961472 | tf_op jit(solution)/shard_map/wtc,wdc->td/dot_general | solution.py:166
  142.6 2.2 collective-permute-start.1
  146.4 1.9 collective-permute-start.2
  148.4 13.0 %collective-permute-done.1 = bf16[80,8192]{1,0:T(8,128)(2,1)S(1)} collective-permute-done((bf16[80,8192]{1,0:T(8,128)(2,1)S(1)}, bf16[80,8192]{1,0:T(8,128)(2,1)S(1)}, u32[]{:S(2)}, u32[]{:S(2)}) %collective-permute-start.1) | collective-permute-done | bytes 1310752 | tf_op jit(solution)/shard_map/ppermute | solution.py:178
  162.7 11.2 %collective-permute-done.2 = bf16[64,8192]{1,0:T(8,128)(2,1)S(1)} collective-permute-done((bf16[64,8192]{1,0:T(8,128)(2,1)S(1)}, bf16[64,8192]{1,0:T(8,128)(2,1)S(1)}, u32[]{:S(2)}, u32[]{:S(2)}) %collective-permute-start.2) | collective-permute-done | bytes 1048608 | tf_op jit(solution)/shard_map/ppermute | solution.py:175
  173.9 2.2 collective-permute-start.3
  177.7 1.9 collective-permute-start.4
  179.6 13.0 %collective-permute-done.3 = bf16[80,8192]{1,0:T(8,128)(2,1)S(1)} collective-permute-done((bf16[80,8192]{1,0:T(8,128)(2,1)S(1)}, bf16[80,8192]{1,0:T(8,128)(2,1)S(1)}, u32[]{:S(2)}, u32[]{:S(2)}) %collective-permute-start.3) | collective-permute-done | bytes 1310752 | tf_op jit(solution)/shard_map/ppermute | solution.py:178
  194.1 14.7 %collective-permute-done.4 = bf16[80,8192]{1,0:T(8,128)(2,1)S(1)} collective-permute-done((bf16[80,8192]{1,0:T(8,128)(2,1)S(1)}, bf16[80,8192]{1,0:T(8,128)(2,1)S(1)}, u32[]{:S(2)}, u32[]{:S(2)}) %collective-permute-start.4) | collective-permute-done | bytes 1310752 | tf_op jit(solution)/shard_map/ppermute | solution.py:175
  208.7 2.2 collective-permute-start.6
  212.9 5.7 %collective-permute-done.6 = bf16[32,8192]{1,0:T(8,128)(2,1)S(1)} collective-permute-done((bf16[32,8192]{1,0:T(8,128)(2,1)S(1)}, bf16[32,8192]{1,0:T(8,128)(2,1)S(1)}, u32[]{:S(2)}, u32[]{:S(2)}) %collective-permute-start.6) | collective-permute-done | bytes 524320 | tf_op jit(solution)/shard_map/ppermute | solution.py:178
  221.2 22.6 %collective-permute-done.7 = bf16[32,8192]{1,0:T(8,128)(2,1)S(1)} collective-permute-done((bf16[32,8192]{1,0:T(8,128)(2,1)S(1)}, bf16[32,8192]{1,0:T(8,128)(2,1)S(1)}, u32[]{:S(2)}, u32[]{:S(2)}) %collective-permute-start.7) | collective-permute-done | bytes 524320 | tf_op jit(solution)/shard_map/ppermute | solution.py:182
  243.8 2.1 maximum_bitcast_fusion
  (69 shorter events, 23.2 us)
Async XLA Ops:
  7.2 7.3 %copy-start.1 = (bf16[1,256,2048]{2,1,0:T(8,128)(2,1)S(1)}, bf16[1,256,2048]{2,1,0:T(8,128)(2,1)}, u32[]{:S(2)}) copy-start(bf16[1,256,2048]{2,1,0:T(8,128)(2,1)} %param.13) | copy-start | bytes 3145732
  7.2 84.5 %all-gather.2.cloned.1.call-start = ((), (), s32[]{:S(2)}) async-start(), calls=%async_computation.1 | async-start | bytes 8912896 | tf_op jit(solution)/shard_map/all_gather | solution.py:86
  10.4 235.6 %reduce-scatter.2.cloned.1.call-start = ((), (), s32[]{:S(2)}) async-start(), calls=%async_computation.2 | async-start | bytes 8912896 | tf_op jit(solution)/shard_map/reduce_scatter | solution.py:135
  20.4 115.8 %copy-start.2 = (f32[256]{0:T(256)}, f32[256]{0:T(256)S(1)}, u32[]{:S(2)}) copy-start(f32[256]{0:T(256)S(1)} %add_rsqrt_fusion) | copy-start | bytes 3076
  118.7 8.4 %copy-start = (bf16[1,256,8192]{2,1,0:T(8,128)(2,1)S(1)}, bf16[1,256,8192]{2,1,0:T(8,128)(2,1)}, u32[]{:S(2)}) copy-start(bf16[1,256,8192]{2,1,0:T(8,128)(2,1)} %param.9) | copy-start | bytes 12582916
  123.8 17.5 %collective-permute-start = (bf16[64,8192]{1,0:T(8,128)(2,1)S(1)}, bf16[64,8192]{1,0:T(8,128)(2,1)S(1)}, u32[]{:S(2)}, u32[]{:S(2)}) collective-permute-start(bf16[64,8192]{1,0:T(8,128)(2,1)S(1)} %fusion.4), channel_id=1, source_target_pairs={{32,33},{33,32},{64,65},{65,64},{96,97},{97,96},{34,35},{35,34},{6... | collective-permute-start | bytes 3145736 | tf_op jit(solution)/shard_map/ppermute | solution.py:178
  136.2 8.7 %slice-start = ((s8[8388608]{0:T(1024)(128)(4,1)}), s8[4194304]{0:T(1024)(128)(4,1)S(1)}, s32[]{:S(2)}) async-start(s8[8388608]{0:T(1024)(128)(4,1)} %bitcast.121), calls=%async_computation.3 | async-start | bytes 8388608
  136.2 8.7 %slice-start.1 = ((s8[8388608]{0:T(1024)(128)(4,1)}), s8[4194304]{0:T(1024)(128)(4,1)S(1)}, s32[]{:S(2)}) async-start(s8[8388608]{0:T(1024)(128)(4,1)} %bitcast.121), calls=%async_computation.4 | async-start | bytes 8388608
  141.3 0.7 slice-start.2
  141.3 3.5 %copy-start.3 = (f32[256]{0:T(256)S(1)}, f32[256]{0:T(256)}, u32[]{:S(2)}) copy-start(f32[256]{0:T(256)} %copy-done.2) | copy-start | bytes 3076
  142.6 18.8 %collective-permute-start.1 = (bf16[80,8192]{1,0:T(8,128)(2,1)S(1)}, bf16[80,8192]{1,0:T(8,128)(2,1)S(1)}, u32[]{:S(2)}, u32[]{:S(2)}) collective-permute-start(bf16[80,8192]{1,0:T(8,128)(2,1)S(1)} %fusion.3), channel_id=1, source_target_pairs={{32,33},{33,32},{64,65},{65,64},{96,97},{97,96},{34,35},{35,34},{6... | collective-permute-start | bytes 3932168 | tf_op jit(solution)/shard_map/ppermute | solution.py:178
  146.4 27.5 %collective-permute-start.2 = (bf16[64,8192]{1,0:T(8,128)(2,1)S(1)}, bf16[64,8192]{1,0:T(8,128)(2,1)S(1)}, u32[]{:S(2)}, u32[]{:S(2)}) collective-permute-start(bf16[64,8192]{1,0:T(8,128)(2,1)S(1)} %multiply_convert_fusion.3), channel_id=1, source_target_pairs={{32,0},{33,1},{65,32},{64,33},{96,64},{97,65},{34,2},{35,3},{67,34... | collective-permute-start | bytes 3145736 | tf_op jit(solution)/shard_map/ppermute | solution.py:175
  173.9 18.7 %collective-permute-start.3 = (bf16[80,8192]{1,0:T(8,128)(2,1)S(1)}, bf16[80,8192]{1,0:T(8,128)(2,1)S(1)}, u32[]{:S(2)}, u32[]{:S(2)}) collective-permute-start(bf16[80,8192]{1,0:T(8,128)(2,1)S(1)} %fusion.2), channel_id=1, source_target_pairs={{32,33},{33,32},{64,65},{65,64},{96,97},{97,96},{34,35},{35,34},{6... | collective-permute-start | bytes 3932168 | tf_op jit(solution)/shard_map/ppermute | solution.py:178
  177.7 31.1 %collective-permute-start.4 = (bf16[80,8192]{1,0:T(8,128)(2,1)S(1)}, bf16[80,8192]{1,0:T(8,128)(2,1)S(1)}, u32[]{:S(2)}, u32[]{:S(2)}) collective-permute-start(bf16[80,8192]{1,0:T(8,128)(2,1)S(1)} %multiply_convert_fusion.2), channel_id=1, source_target_pairs={{32,0},{33,1},{65,32},{64,33},{96,64},{97,65},{34,2},{35,3},{67,34... | collective-permute-start | bytes 3932168 | tf_op jit(solution)/shard_map/ppermute | solution.py:175
  208.7 9.9 %collective-permute-start.6 = (bf16[32,8192]{1,0:T(8,128)(2,1)S(1)}, bf16[32,8192]{1,0:T(8,128)(2,1)S(1)}, u32[]{:S(2)}, u32[]{:S(2)}) collective-permute-start(bf16[32,8192]{1,0:T(8,128)(2,1)S(1)} %fusion.5), channel_id=1, source_target_pairs={{32,33},{33,32},{64,65},{65,64},{96,97},{97,96},{34,35},{35,34},{6... | collective-permute-start | bytes 1572872 | tf_op jit(solution)/shard_map/ppermute | solution.py:178
  211.0 32.8 %collective-permute-start.5 = (bf16[80,8192]{1,0:T(8,128)(2,1)S(1)}, bf16[80,8192]{1,0:T(8,128)(2,1)S(1)}, u32[]{:S(2)}, u32[]{:S(2)}) collective-permute-start(bf16[80,8192]{1,0:T(8,128)(2,1)S(1)} %multiply_convert_fusion.1), channel_id=1, source_target_pairs={{32,0},{33,1},{65,32},{64,33},{96,64},{97,65},{34,2},{35,3},{67,34... | collective-permute-start | bytes 3932168 | tf_op jit(solution)/shard_map/ppermute | solution.py:175
  219.3 24.5 %collective-permute-start.7 = (bf16[32,8192]{1,0:T(8,128)(2,1)S(1)}, bf16[32,8192]{1,0:T(8,128)(2,1)S(1)}, u32[]{:S(2)}, u32[]{:S(2)}) collective-permute-start(bf16[32,8192]{1,0:T(8,128)(2,1)S(1)} %multiply_convert_fusion.7), channel_id=1, source_target_pairs={{32,0},{33,1},{65,32},{64,33},{96,64},{97,65},{34,2},{35,3},{67,34... | collective-permute-start | bytes 1572872 | tf_op jit(solution)/shard_map/ppermute | solution.py:182
Sparse Core Ops, SparseCore 0:
  10.7 80.9 all-gather.1
  133.0 84.3 reduce-scatter.1
where the time goes:
time: 255 us
  waiting for transfers between devices  151 us (59%)
  matrix products  44.6 us (17%)
  starting transfers between devices  17.6 us (7%)
  between operations  16.5 us (6%)
  other arithmetic  16 us (6%)
  local copies, waits for them, and re-layouts  8.69 us (3%)
    all_gather x1, waiting for transfers between devices, on_device(): lax.all_gather(jnp.stack([key_weight[0], value_weight[0]]), 'dp', axis=1,...  71.1 us
    ppermute x4, waiting for transfers between devices, on_device(): lowers.append(lax.ppermute(held, ('pipe', 'tensor'), shift_pairs))  48.4 us
    ppermute x4, waiting for transfers between devices, on_device(): lax.ppermute(part_low, ('pipe', 'tensor'), pairs).astype(jnp.float32)  31.7 us
    dot_general x4, matrix products, on_device(): jnp.einsum('wtc,wdc->td', both_grads[:, sl], both_full, preferred_element...  13.3 us
    ppermute x4, starting transfers between devices, on_device(): lax.ppermute(part_low, ('pipe', 'tensor'), pairs).astype(jnp.float32)  9.85 us
    ppermute x4, starting transfers between devices, on_device(): lowers.append(lax.ppermute(held, ('pipe', 'tensor'), shift_pairs))  7.67 us
    dot_general x1, matrix products, sequence_grads(): jnp.einsum('kgij,ikgd->jkd', score_grad, query_g, preferred_element_type=...  7.48 us
    dot_general x1, matrix products, on_device(): jnp.einsum('td,wdc->wtc', normed, both_full, preferred_element_type=jnp.f...  7.02 us
  transfers between devices with their start and end apart: 10, of which 7 were waited for; matrix products, arithmetic and copies ran while one was open for 13% of the time, Pallas kernels for 0%

commit v1 on v0

--- a/solution.py
+++ b/solution.py
@@ -8,6 +8,13 @@
 npo_beta = 0.1
 norm_eps = 1e-05
 rope_base = 500000.0
+
+
+def exchange_gather(array, axis, along):
+    n_dev = lax.axis_size(axis)
+    blocks = jnp.stack([array for _ in range(n_dev)])
+    blocks = lax.all_to_all(blocks, axis, split_axis=0, concat_axis=0)
+    return jnp.concatenate(blocks, axis=along)
 
 
 def shifted(value, axis, steps):
@@ -83,9 +90,7 @@
     policy_logp,
     reference_logp,
 ):
-    both_full = lax.all_gather(
-        jnp.stack([key_weight[0], value_weight[0]]), "dp", axis=1, tiled=True
-    )
+    both_full = exchange_gather(jnp.stack([key_weight[0], value_weight[0]]), "dp", 1)
     key_full, value_full = (both_full[0], both_full[1])
     hidden = hidden_states[0]
     gain_f = norm_gain[0].astype(jnp.float32)

time: 255 us -> 338 us (1.33)
  waiting for transfers between devices: 151 us -> 213 us
  local copies, waits for them, and re-layouts: 8.69 us -> 20.2 us
  starting transfers between devices: 17.6 us -> 26.6 us
    all_to_all x0 -> x1, waiting for transfers between devices: none -> 135 us  [exchange_gather(): blocks = lax.all_to_all(blocks, axis, split_axis=0, concat_axis=0)]
    all_gather x1 -> x0, waiting for transfers between devices: 71.1 us -> none  [on_device(): lax.all_gather(jnp.stack([key_weight[0], value_weight[0]]), 'dp', axis=1,...]
    all_to_all x0 -> x1, starting transfers between devices: none -> 8.78 us  [exchange_gather(): blocks = lax.all_to_all(blocks, axis, split_axis=0, concat_axis=0)]
    reshape x0 -> x1, local copies, waits for them, and re-layouts: none -> 8 us  [exchange_gather(): return jnp.concatenate(blocks, axis=along)]
    another operation x0 -> x2, local copies, waits for them, and re-layouts: none -> 4.4 us  [the longest x1 4.19 us: exchange_gather(): blocks = jnp.stack([array for _ in range(n_dev)])]
  transfers between devices with their start and end apart: 10 -> 10, of which waited for: 7 -> 7; matrix products, arithmetic and copies ran while one was open for 13% -> 10% of each run, Pallas kernels for 0% -> 0%
where the time goes in v1:
time: 338 us; the launch traced here: 336 us
  waiting for transfers between devices  213 us (63%)
  matrix products  43.5 us (13%)
  starting transfers between devices  26.6 us (8%)
  local copies, waits for them, and re-layouts  20.2 us (6%)
  between operations  16.5 us (5%)
  other arithmetic  15.7 us (5%)
    all_to_all x1, waiting for transfers between devices, exchange_gather(): blocks = lax.all_to_all(blocks, axis, split_axis=0, concat_axis=0)  135 us
    ppermute x4, waiting for transfers between devices, on_device(): lowers.append(lax.ppermute(held, ('pipe', 'tensor'), shift_pairs))  45.8 us
    ppermute x4, waiting for transfers between devices, on_device(): lax.ppermute(part_low, ('pipe', 'tensor'), pairs).astype(jnp.float32)  31.9 us
    dot_general x4, matrix products, on_device(): jnp.einsum('wtc,wdc->td', both_grads[:, sl], both_full, preferred_element...  13.3 us
    ppermute x4, starting transfers between devices, on_device(): lax.ppermute(part_low, ('pipe', 'tensor'), pairs).astype(jnp.float32)  10.2 us
    all_to_all x1, starting transfers between devices, exchange_gather(): blocks = lax.all_to_all(blocks, axis, split_axis=0, concat_axis=0)  8.78 us
    reshape x1, local copies, waits for them, and re-layouts, exchange_gather(): return jnp.concatenate(blocks, axis=along)  8 us
    ppermute x4, starting transfers between devices, on_device(): lowers.append(lax.ppermute(held, ('pipe', 'tensor'), shift_pairs))  7.67 us
  transfers between devices with their start and end apart: 10, of which 7 were waited for; matrix products, arithmetic and copies ran while one was open for 10% of the time, Pallas kernels for 0%

profile of v1, /device:TPU:1, one launch (start us, length us, event | category | flops | bytes accessed | tf_op | source)
XLA Modules:
  0.0 335.8 jit_solution(13456269614851034239)
XLA Ops:
  8.5 4.2 %stack.7 = bf16[16,2,512,256]{2,3,1,0:T(8,128)(2,1)} broadcast(bf16[2,512,256]{1,2,0:T(8,128)(2,1)S(1)} %copy.31), dimensions={1,2,3} | broadcast | bytes 8912896 | tf_op jit(solution)/shard_map/stack | solution.py:15
  12.7 8.8 %all-to-all-start = ((bf16[16,2,512,256]{2,3,1,0:T(8,128)(2,1)}), bf16[16,2,512,256]{2,3,1,0:T(8,128)(2,1)}, u32[]{:S(2)}, u32[]{:S(2)}) async-start(bf16[16,2,512,256]{2,3,1,0:T(8,128)(2,1)} %stack.7), calls=%async_computation | async-start | bytes 16777216 | tf_op jit(solution)/shard_map/all_to_all | solution.py:16
  28.2 3.1 fusion.8
  32.1 135.5 %all-to-all-done = bf16[16,2,512,256]{2,3,1,0:T(8,128)(2,1)} async-done(((bf16[16,2,512,256]{2,3,1,0:T(8,128)(2,1)}), bf16[16,2,512,256]{2,3,1,0:T(8,128)(2,1)}, u32[]{:S(2)}, u32[]{:S(2)}) %all-to-all-start) | async-done | bytes 8388640 | tf_op jit(solution)/shard_map/all_to_all | solution.py:16
  167.6 8.0 %copy.68 = bf16[16,2,32,8,512]{4,3,0,2,1:T(8,128)(2,1)} copy(bf16[16,2,32,8,512]{4,3,2,1,0:T(8,128)(2,1)} %bitcast.44) | data formatting | bytes 16777216 | tf_op jit(solution)/shard_map/reshape | solution.py:17
  175.6 5.8 %fusion.28 = f32[2,256,256]{1,2,0:T(8,128)S(1)} fusion(bf16[2,8192,256]{1,2,0:T(8,128)(2,1)} %bitcast.126, bf16[1,256,8192]{2,1,0:T(8,128)(2,1)S(1)} %copy-done, f32[8192]{0:T(1024)S(1)} %bitcast.135, f32[256]{0:T(256)S(1)} %add_rsqrt_fusion), kind=kOutput, calls=%fused_computation.51 | convolution fusion | flops 2155872256 | bytes 13140992 | tf_op jit(solution)/shard_map/td,wdc->wtc/dot_general | solution.py:107
  182.6 5.3 %fusion.69 = (f32[2,8,256]{2,1,0:T(8,128)S(1)}, f32[2,8,256,256]{2,3,1,0:T(8,128)}) fusion(pred[256,256]{0,1:T(8,128)(4,1)} %fusion.47, bf16[256,2,8,128]{0,3,2,1:T(8,128)(2,1)} %bitcast.147, f32[256,2,64]{2,0,1:T(8,128)S(1)} %bitcast.152, f32[256,2,64]{2,0,1:T(8,128)} %negate_bitcast_fusion, f32[256,2,128]{2,0,1:T(8,128)S(1)} %copy.34, ...), kind=kOutput, calls=%fused_computation.114 | convolution fusion | flops 274006272 | bytes 6111232 | tf_op jit(solution)/shard_map/while/body/eval_jaxpr/sub | solution.py:60
  187.9 3.1 fusion.35
  191.6 2.7 fusion.38
  194.4 7.5 %fusion.31 = f32[2,256,128]{1,2,0:T(8,128)S(1)} fusion(bf16[256,2,8,128]{0,3,2,1:T(8,128)(2,1)} %bitcast.148, f32[2,256,256,8]{2,1,3,0:T(8,128)} %fusion.38, f32[2,8,256,256]{2,3,1,0:T(8,128)} %get-tuple-element.60, f32[2,8,256]{2,1,0:T(8,128)S(1)} %get-tuple-element.59), kind=kOutput, calls=%fused_computation.52 | convolution fusion | flops 275779840 | bytes 9715712 | tf_op jit(solution)/shard_map/while/body/eval_jaxpr/kgij,ikgd->jkd/dot_general | solution.py:69
  202.1 5.1 %fusion.6 = bf16[64,8192]{1,0:T(8,128)(2,1)S(1)} fusion(bf16[2,8192,256]{1,2,0:T(8,128)(2,1)} %bitcast.127, bf16[1,256,256]{2,1,0:T(8,128)(2,1)S(1)} %copy.45, bf16[1,256,256]{2,1,0:T(8,128)(2,1)S(1)} %copy.46), kind=kOutput, calls=%fused_computation.12 | convolution fusion | flops 537427968 | bytes 9699328 | tf_op jit(solution)/shard_map/wtc,wdc->td/dot_general | solution.py:171
  207.2 3.3 collective-permute-start
  210.5 5.8 %convolution_convert_fusion = bf16[8192,512]{1,0:T(8,128)(2,1)} fusion(f32[8192]{0:T(1024)S(1)} %bitcast.136, bf16[256,256]{0,1:T(8,128)(2,1)S(1)} %bitcast.154, bf16[256,256]{0,1:T(8,128)(2,1)S(1)} %bitcast.151, bf16[1,256,8192]{2,1,0:T(8,128)(2,1)S(1)} %copy-done.1, f32[256]{0:T(256)S(1)} %add_rsqrt_fusion), kind=kOutput, calls=%fused_computation.2 | convolution fusion | flops 2160590848 | bytes 12878848 | tf_op jit(solution)/shard_map/dot_general | solution.py:141
  216.4 3.3 fusion.2
  219.7 5.1 %fusion.5 = bf16[80,8192]{1,0:T(8,128)(2,1)S(1)} fusion(bf16[2,8192,256]{1,2,0:T(8,128)(2,1)} %bitcast.128, bf16[1,256,256]{2,1,0:T(8,128)(2,1)S(1)} %copy.45, bf16[1,256,256]{2,1,0:T(8,128)(2,1)S(1)} %copy.46), kind=kOutput, calls=%fused_computation.11 | convolution fusion | flops 671784960 | bytes 9961472 | tf_op jit(solution)/shard_map/wtc,wdc->td/dot_general | solution.py:171
  226.1 2.2 collective-permute-start.1
  231.9 13.0 %collective-permute-done.1 = bf16[80,8192]{1,0:T(8,128)(2,1)S(1)} collective-permute-done((bf16[80,8192]{1,0:T(8,128)(2,1)S(1)}, bf16[80,8192]{1,0:T(8,128)(2,1)S(1)}, u32[]{:S(2)}, u32[]{:S(2)}) %collective-permute-start.1) | collective-permute-done | bytes 1310752 | tf_op jit(solution)/shard_map/ppermute | solution.py:183
  246.2 10.8 %collective-permute-done.2 = bf16[64,8192]{1,0:T(8,128)(2,1)S(1)} collective-permute-done((bf16[64,8192]{1,0:T(8,128)(2,1)S(1)}, bf16[64,8192]{1,0:T(8,128)(2,1)S(1)}, u32[]{:S(2)}, u32[]{:S(2)}) %collective-permute-start.2) | collective-permute-done | bytes 1048608 | tf_op jit(solution)/shard_map/ppermute | solution.py:180
  257.0 2.5 collective-permute-start.3
  263.0 12.7 %collective-permute-done.3 = bf16[80,8192]{1,0:T(8,128)(2,1)S(1)} collective-permute-done((bf16[80,8192]{1,0:T(8,128)(2,1)S(1)}, bf16[80,8192]{1,0:T(8,128)(2,1)S(1)}, u32[]{:S(2)}, u32[]{:S(2)}) %collective-permute-start.3) | collective-permute-done | bytes 1310752 | tf_op jit(solution)/shard_map/ppermute | solution.py:183
  277.1 13.6 %collective-permute-done.4 = bf16[80,8192]{1,0:T(8,128)(2,1)S(1)} collective-permute-done((bf16[80,8192]{1,0:T(8,128)(2,1)S(1)}, bf16[80,8192]{1,0:T(8,128)(2,1)S(1)}, u32[]{:S(2)}, u32[]{:S(2)}) %collective-permute-start.4) | collective-permute-done | bytes 1310752 | tf_op jit(solution)/shard_map/ppermute | solution.py:180
  290.6 2.2 collective-permute-start.6
  294.8 6.1 %collective-permute-done.6 = bf16[32,8192]{1,0:T(8,128)(2,1)S(1)} collective-permute-done((bf16[32,8192]{1,0:T(8,128)(2,1)S(1)}, bf16[32,8192]{1,0:T(8,128)(2,1)S(1)}, u32[]{:S(2)}, u32[]{:S(2)}) %collective-permute-start.6) | collective-permute-done | bytes 524320 | tf_op jit(solution)/shard_map/ppermute | solution.py:183
  303.5 21.4 %collective-permute-done.7 = bf16[32,8192]{1,0:T(8,128)(2,1)S(1)} collective-permute-done((bf16[32,8192]{1,0:T(8,128)(2,1)S(1)}, bf16[32,8192]{1,0:T(8,128)(2,1)S(1)}, u32[]{:S(2)}, u32[]{:S(2)}) %collective-permute-start.7) | collective-permute-done | bytes 524320 | tf_op jit(solution)/shard_map/ppermute | solution.py:187
  (77 shorter events, 28.2 us)
Async XLA Ops:
  12.7 10.9 %copy-start.5 = (bf16[1,8192]{1,0:T(2,128)(2,1)S(1)}, bf16[1,8192]{1,0:T(2,128)(2,1)}, u32[]{:S(2)}) copy-start(bf16[1,8192]{1,0:T(2,128)(2,1)} %param.10) | copy-start | bytes 49156
  12.7 12.8 %copy-start.2 = (bf16[1,256,2048]{2,1,0:T(8,128)(2,1)S(1)}, bf16[1,256,2048]{2,1,0:T(8,128)(2,1)}, u32[]{:S(2)}) copy-start(bf16[1,256,2048]{2,1,0:T(8,128)(2,1)} %param.13) | copy-start | bytes 3145732
  12.7 154.9 %all-to-all-start = ((bf16[16,2,512,256]{2,3,1,0:T(8,128)(2,1)}), bf16[16,2,512,256]{2,3,1,0:T(8,128)(2,1)}, u32[]{:S(2)}, u32[]{:S(2)}) async-start(bf16[16,2,512,256]{2,3,1,0:T(8,128)(2,1)} %stack.7), calls=%async_computation | async-start | bytes 16777216 | tf_op jit(solution)/shard_map/all_to_all | solution.py:16
  21.4 305.6 %reduce-scatter.2.cloned.1.call-start = ((), (), s32[]{:S(2)}) async-start(), calls=%async_computation.2 | async-start | bytes 8912896 | tf_op jit(solution)/shard_map/reduce_scatter | solution.py:140
  31.4 188.3 %copy-start.6 = (f32[256]{0:T(256)}, f32[256]{0:T(256)S(1)}, u32[]{:S(2)}) copy-start(f32[256]{0:T(256)S(1)} %add_rsqrt_fusion) | copy-start | bytes 3076
  167.6 8.0 %copy-start = (bf16[1,256,8192]{2,1,0:T(8,128)(2,1)S(1)}, bf16[1,256,8192]{2,1,0:T(8,128)(2,1)}, u32[]{:S(2)}) copy-start(bf16[1,256,8192]{2,1,0:T(8,128)(2,1)} %param.9) | copy-start | bytes 12582916
  191.0 0.7 copy-start.3
  202.1 8.4 %copy-start.1 = (bf16[1,256,8192]{2,1,0:T(8,128)(2,1)S(1)}, bf16[1,256,8192]{2,1,0:T(8,128)(2,1)}, u32[]{:S(2)}) copy-start(bf16[1,256,8192]{2,1,0:T(8,128)(2,1)} %param.9) | copy-start | bytes 12582916
  202.1 8.4 %copy-start.4 = (bf16[2,128,256]{2,1,0:T(8,128)(2,1)S(1)}, bf16[2,128,256]{2,1,0:T(8,128)(2,1)}, u32[]{:S(2)}) copy-start(bf16[2,128,256]{2,1,0:T(8,128)(2,1)} %copy-done.3) | copy-start | bytes 393220
  207.2 17.6 %collective-permute-start = (bf16[64,8192]{1,0:T(8,128)(2,1)S(1)}, bf16[64,8192]{1,0:T(8,128)(2,1)S(1)}, u32[]{:S(2)}, u32[]{:S(2)}) collective-permute-start(bf16[64,8192]{1,0:T(8,128)(2,1)S(1)} %fusion.6), channel_id=1, source_target_pairs={{32,33},{33,32},{64,65},{65,64},{96,97},{97,96},{34,35},{35,34},{6... | collective-permute-start | bytes 3145736 | tf_op jit(solution)/shard_map/ppermute | solution.py:183
  219.7 8.8 %slice-start = ((s8[8388608]{0:T(1024)(128)(4,1)}), s8[4194304]{0:T(1024)(128)(4,1)S(1)}, s32[]{:S(2)}) async-start(s8[8388608]{0:T(1024)(128)(4,1)} %bitcast.129), calls=%async_computation.3 | async-start | bytes 8388608
  219.7 8.7 %slice-start.1 = ((s8[8388608]{0:T(1024)(128)(4,1)}), s8[4194304]{0:T(1024)(128)(4,1)S(1)}, s32[]{:S(2)}) async-start(s8[8388608]{0:T(1024)(128)(4,1)} %bitcast.129), calls=%async_computation.4 | async-start | bytes 8388608
  224.8 0.8 slice-start.2
  224.8 3.5 %copy-start.7 = (f32[256]{0:T(256)S(1)}, f32[256]{0:T(256)}, u32[]{:S(2)}) copy-start(f32[256]{0:T(256)} %copy-done.6) | copy-start | bytes 3076
  226.1 18.8 %collective-permute-start.1 = (bf16[80,8192]{1,0:T(8,128)(2,1)S(1)}, bf16[80,8192]{1,0:T(8,128)(2,1)S(1)}, u32[]{:S(2)}, u32[]{:S(2)}) collective-permute-start(bf16[80,8192]{1,0:T(8,128)(2,1)S(1)} %fusion.5), channel_id=1, source_target_pairs={{32,33},{33,32},{64,65},{65,64},{96,97},{97,96},{34,35},{35,34},{6... | collective-permute-start | bytes 3932168 | tf_op jit(solution)/shard_map/ppermute | solution.py:183
  230.0 27.0 %collective-permute-start.2 = (bf16[64,8192]{1,0:T(8,128)(2,1)S(1)}, bf16[64,8192]{1,0:T(8,128)(2,1)S(1)}, u32[]{:S(2)}, u32[]{:S(2)}) collective-permute-start(bf16[64,8192]{1,0:T(8,128)(2,1)S(1)} %multiply_convert_fusion.4), channel_id=1, source_target_pairs={{32,0},{33,1},{65,32},{64,33},{96,64},{97,65},{34,2},{35,3},{67,34... | collective-permute-start | bytes 3145736 | tf_op jit(solution)/shard_map/ppermute | solution.py:180
  257.0 18.7 %collective-permute-start.3 = (bf16[80,8192]{1,0:T(8,128)(2,1)S(1)}, bf16[80,8192]{1,0:T(8,128)(2,1)S(1)}, u32[]{:S(2)}, u32[]{:S(2)}) collective-permute-start(bf16[80,8192]{1,0:T(8,128)(2,1)S(1)} %fusion.4), channel_id=1, source_target_pairs={{32,33},{33,32},{64,65},{65,64},{96,97},{97,96},{34,35},{35,34},{6... | collective-permute-start | bytes 3932168 | tf_op jit(solution)/shard_map/ppermute | solution.py:183
  261.1 29.5 %collective-permute-start.4 = (bf16[80,8192]{1,0:T(8,128)(2,1)S(1)}, bf16[80,8192]{1,0:T(8,128)(2,1)S(1)}, u32[]{:S(2)}, u32[]{:S(2)}) collective-permute-start(bf16[80,8192]{1,0:T(8,128)(2,1)S(1)} %multiply_convert_fusion.3), channel_id=1, source_target_pairs={{32,0},{33,1},{65,32},{64,33},{96,64},{97,65},{34,2},{35,3},{67,34... | collective-permute-start | bytes 3932168 | tf_op jit(solution)/shard_map/ppermute | solution.py:180
  290.6 10.3 %collective-permute-start.6 = (bf16[32,8192]{1,0:T(8,128)(2,1)S(1)}, bf16[32,8192]{1,0:T(8,128)(2,1)S(1)}, u32[]{:S(2)}, u32[]{:S(2)}) collective-permute-start(bf16[32,8192]{1,0:T(8,128)(2,1)S(1)} %fusion.7), channel_id=1, source_target_pairs={{32,33},{33,32},{64,65},{65,64},{96,97},{97,96},{34,35},{35,34},{6... | collective-permute-start | bytes 1572872 | tf_op jit(solution)/shard_map/ppermute | solution.py:183
  292.9 32.0 %collective-permute-start.5 = (bf16[80,8192]{1,0:T(8,128)(2,1)S(1)}, bf16[80,8192]{1,0:T(8,128)(2,1)S(1)}, u32[]{:S(2)}, u32[]{:S(2)}) collective-permute-start(bf16[80,8192]{1,0:T(8,128)(2,1)S(1)} %multiply_convert_fusion.2), channel_id=1, source_target_pairs={{32,0},{33,1},{65,32},{64,33},{96,64},{97,65},{34,2},{35,3},{67,34... | collective-permute-start | bytes 3932168 | tf_op jit(solution)/shard_map/ppermute | solution.py:180
  301.5 23.4 %collective-permute-start.7 = (bf16[32,8192]{1,0:T(8,128)(2,1)S(1)}, bf16[32,8192]{1,0:T(8,128)(2,1)S(1)}, u32[]{:S(2)}, u32[]{:S(2)}) collective-permute-start(bf16[32,8192]{1,0:T(8,128)(2,1)S(1)} %multiply_convert_fusion.6), channel_id=1, source_target_pairs={{32,0},{33,1},{65,32},{64,33},{96,64},{97,65},{34,2},{35,3},{67,34... | collective-permute-start | bytes 1572872 | tf_op jit(solution)/shard_map/ppermute | solution.py:187
Sparse Core Ops, SparseCore 0:
  216.5 88.5 reduce-scatter.1
